TPU v7x, 256 devices: a whole 4x4x8 slice. The times are simulated.
256 devices in a mesh: sec: 16 (over y, x), bulk: 16 (over z, core).
Axes of the slice: x: 4, y: 4, z: 8, core: 2. Of those that a mesh axis runs over, the one named last changes fastest.
Arguments:
- modes_x: bfloat16 [96, 16, 64, 8, 128], P(None, 'sec', 'bulk'), may hold values from -30 to 30
- modes_p: bfloat16 [96, 16, 64, 8, 128], P(None, 'sec', 'bulk'), may hold values from -30 to 30
- ritz_values: float32 [96], replicated, may hold values from 0.05 to 2
- node_types: int32 [16, 64, 8, 128], P('sec', 'bulk'), may hold values from 0 to 7
- stiff_table: float32 [8], replicated, may hold values from 1 to 10
- mass_table: float32 [8], replicated, may hold values from 0.5 to 4
- joint_nodes: int32 [16, 16, 16, 128], P('sec', 'bulk'), may hold values from 0 to 4095
- joint_count: int32 [16, 16, 16], P('sec', 'bulk'), may hold values from 0 to 128, as said below
Outputs:
- search_dir: bfloat16 [96, 16, 64, 8, 128], P(None, 'sec', 'bulk')
- ritz_pencil: float32 [288, 288], replicated
Inputs may be any that keep to these rules, and one draw needn't show every extreme that they name: `joint_nodes`: local node numbers of a slab; slots at or beyond the count are ignored; a node may appear in several slots. Symmetric: joint_count[a, b, c] = joint_count[c, b, a], zero for a = c.
All inputs are finite; a program needn't handle non-finite values.
Results may differ from a plain program's by a relative error of at most 0.0004.
The roundings to bfloat16 on the way count: a program that leaves them out, or rounds other values in their place, can miss the bound.
Values may be sent and summed in bfloat16 or wider, within the bound.
No kernel may reach another device: no remote copies, remote signals or barrier semaphores. Data moves between devices by JAX's collectives and lax.ppermute only.
A program may use at most 64 MiB of HBM per device.

v0:
```python
import jax
import jax.numpy as jnp
from jax import lax
from jax.sharding import PartitionSpec as P

JOINT_GAIN = 0.5
SPRING = (0.0, 0.1, 0.05, 0.025)
OFFSETS = [
    (step_z, step_y, step_x)
    for step_z in (-1, 0, 1)
    for step_y in (-1, 0, 1)
    for step_x in (-1, 0, 1)
    if (step_z, step_y, step_x) != (0, 0, 0)
]


def extended(shard, sides, width):
    for axis, dim in sides:
        peers, length = (lax.axis_size(axis), shard.shape[dim])
        up = [(i, (i + 1) % peers) for i in range(peers - 1)]
        down = [(j, i) for i, j in up]
        last = lax.slice_in_dim(shard, length - width, length, axis=dim)
        first = lax.slice_in_dim(shard, 0, width, axis=dim)
        before = lax.ppermute(last, axis, up)
        after = lax.ppermute(first, axis, down)
        shard = jnp.concatenate([before, shard, after], axis=dim)
    return shard


def lower_solve(lower, matrix):
    return lax.linalg.triangular_solve(lower, matrix, left_side=True, lower=True)


def edge_weights(kappa_pad):
    padded = jnp.pad(kappa_pad.astype(jnp.float32), ((0, 0), (1, 1), (1, 1)))
    depth = padded.shape[0] - 2
    height = padded.shape[1] - 2
    breadth = padded.shape[2] - 2
    centre = padded[1:-1, 1:-1, 1:-1]
    weights = []
    summed = jnp.zeros(centre.shape, jnp.float32)
    for offset in OFFSETS:
        step_z, step_y, step_x = offset
        other = padded[
            1 + step_z : 1 + step_z + depth,
            1 + step_y : 1 + step_y + height,
            1 + step_x : 1 + step_x + breadth,
        ]
        reach = abs(step_z) + abs(step_y) + abs(step_x)
        weight = SPRING[reach] * 2.0 * centre * other / (centre + other)
        weights.append(weight)
        summed = summed + weight
    return (weights, summed)


def apply_stencil(values_pad, weights, summed):
    padded = jnp.pad(values_pad, ((0, 0), (0, 0), (1, 1), (1, 1)))
    depth = padded.shape[1] - 2
    height = padded.shape[2] - 2
    breadth = padded.shape[3] - 2
    accum = jnp.zeros((padded.shape[0], depth, height, breadth), jnp.float32)
    for offset, weight in zip(OFFSETS, weights):
        step_z, step_y, step_x = offset
        other = padded[
            :,
            1 + step_z : 1 + step_z + depth,
            1 + step_y : 1 + step_y + height,
            1 + step_x : 1 + step_x + breadth,
        ]
        accum = accum + weight[None] * other.astype(jnp.float32)
    centre = padded[:, 1:-1, 1:-1, 1:-1].astype(jnp.float32)
    return summed[None] * centre - accum


def joint_apply(result, sent, recv, node_ids, joint_w):
    width = result.shape[0]
    delta = joint_w.reshape(1, -1) * (sent.astype(jnp.float32) - recv.astype(jnp.float32)).reshape(
        width, -1
    )
    return result.reshape(width, -1).at[:, node_ids].add(delta).reshape(result.shape)


def upper_blocks(rows, cols, width):
    contract = (((1,), (1,)), ((), ()))
    parts = []
    for index in range(rows.shape[0] // width):
        part = lax.dot_general(
            rows[index * width : (index + 1) * width],
            cols[index * width :],
            contract,
            preferred_element_type=jnp.float32,
        )
        parts.append(part)
    return jnp.concatenate(parts, axis=1)


def unpack_blocks(packed, width):
    blocks = 0
    while width * blocks * (blocks + 1) // 2 < packed.shape[1]:
        blocks += 1
    offset = 0
    rows = []
    for index in range(blocks):
        span = (blocks - index) * width
        gap = jnp.zeros((width, index * width), packed.dtype)
        rows.append(jnp.concatenate([gap, packed[:, offset : offset + span]], axis=1))
        offset += span
    return jnp.concatenate(rows, axis=0)


def mirror(matrix):
    return jnp.triu(matrix) + jnp.transpose(jnp.triu(matrix, 1))


def fetch(block, node_ids, sections, capacity):
    padded = extended(block, (("bulk", 1),), 1)
    width = block.shape[0]
    sent = jnp.take(block.reshape(width, -1), node_ids, axis=1).reshape(width, sections, capacity)
    recv = lax.all_to_all(sent, "sec", split_axis=1, concat_axis=1, tiled=True)
    return (padded, sent, recv)


def on_device(
    modes_x, modes_p, ritz_values, node_types, stiff_table, mass_table, joint_nodes, joint_count
):
    modes = modes_x.shape[0]
    sections = joint_nodes.shape[2]
    capacity = joint_nodes.shape[3]
    columns = 3 * modes
    levels = jnp.arange(stiff_table.shape[0], dtype=jnp.int32)[:, None, None, None]
    chosen = node_types[0][None] == levels
    kappa = jnp.sum(jnp.where(chosen, stiff_table[:, None, None, None], 0.0), axis=0).astype(
        jnp.bfloat16
    )
    mass = jnp.sum(jnp.where(chosen, mass_table[:, None, None, None], 0.0), axis=0)
    node_ids = joint_nodes[0, 0].reshape(-1)
    live = (jnp.arange(capacity, dtype=jnp.int32)[None, :] < joint_count[0, 0][:, None]).astype(
        jnp.float32
    )
    x_local = modes_x[:, 0]
    p_local = modes_p[:, 0]
    k_row = x_local.shape[0]
    first = jnp.concatenate([x_local, kappa[None]], axis=0)
    padded, sent, recv = fetch(first, node_ids, sections, capacity)
    weights, summed = edge_weights(padded[k_row])
    own = sent[k_row].astype(jnp.float32)
    other = recv[k_row].astype(jnp.float32)
    joint_w = JOINT_GAIN * 2.0 * own * other / (own + other) * live
    diag_full = summed.reshape(-1).at[node_ids].add(joint_w.reshape(-1)).reshape(summed.shape)
    stiff_first = joint_apply(
        apply_stencil(padded[:k_row], weights, summed),
        sent[:k_row],
        recv[:k_row],
        node_ids,
        joint_w,
    )
    resid = (
        stiff_first - mass[None] * x_local.astype(jnp.float32) * ritz_values[:, None, None, None]
    )
    search_local = (resid / diag_full[None]).astype(jnp.bfloat16)
    second = jnp.concatenate([search_local, p_local], axis=0)
    padded_two, sent_two, recv_two = fetch(second, node_ids, sections, capacity)
    stiff_wp = joint_apply(
        apply_stencil(padded_two, weights, summed), sent_two, recv_two, node_ids, joint_w
    )
    span = jnp.concatenate([x_local, second], axis=0).reshape(columns, -1)
    stiff_span = (
        jnp.concatenate([stiff_first, stiff_wp], axis=0).astype(jnp.bfloat16).reshape(columns, -1)
    )
    mass_span = (mass.reshape(1, -1) * span.astype(jnp.float32)).astype(jnp.bfloat16)
    gram_m = lax.psum(lax.psum(upper_blocks(span, mass_span, modes), "bulk"), "sec")
    stiff_part = upper_blocks(span, stiff_span, modes)
    gram_m, stiff_part = lax.optimization_barrier((gram_m, stiff_part))
    gram_k = lax.psum(lax.psum(stiff_part, "bulk"), "sec")
    mass_gram = mirror(unpack_blocks(gram_m, modes))
    stiff_gram = mirror(unpack_blocks(gram_k, modes))
    lower = jnp.linalg.cholesky(mass_gram)
    inverse = lower_solve(lower, jnp.eye(columns, dtype=jnp.float32))
    exact = lax.Precision.HIGHEST
    half = jnp.matmul(inverse, stiff_gram, precision=exact)
    ritz_pencil = jnp.matmul(half, jnp.transpose(inverse), precision=exact)
    return (search_local[:, None], ritz_pencil)


def solution(mesh):
    placed = (
        P(None, "sec", "bulk", None, None),
        P(None, "sec", "bulk", None, None),
        P(),
        P("sec", "bulk", None, None),
        P(),
        P(),
        P("sec", "bulk", None, None),
        P("sec", "bulk", None),
    )
    return jax.shard_map(
        on_device,
        mesh=mesh,
        in_specs=placed,
        out_specs=(P(None, "sec", "bulk", None, None), P()),
        check_vma=False,
    )
```

profile of v0, /device:TPU:32, one launch (start us, length us, event | category | flops | bytes accessed | tf_op | source)
XLA Modules:
  0.0 560.2 jit_solution(6228942137165287355)
XLA Ops:
  14.2 3.2 convert_element_type.358
  20.4 6.2 %gather_fusion = bf16[2048,97]{1,0:T(8,128)(2,1)S(1)} fusion(bf16[97,4096]{0,1:T(8,128)(2,1)S(1)} %pad_maximum_fusion.6, s32[2048]{0:T(1024)S(1)} %broadcast_clamp_fusion), kind=kCustom, calls=%fused_computation | custom fusion | bytes 802816 | tf_op jit(solution)/shard_map/jit(_take)/gather | solution.py:118
  27.8 7.1 %all-to-all-start = ((bf16[97,16,128]{2,0,1:T(8,128)(2,1)}), bf16[97,16,128]{2,0,1:T(8,128)(2,1)}, u32[]{:S(2)}, u32[]{:S(2)}) async-start(bf16[97,16,128]{2,0,1:T(8,128)(2,1)} %broadcast_select_fusion.1), calls=%async_computation | async-start | bytes 851968 | tf_op jit(solution)/shard_map/all_to_all | solution.py:119
  44.6 8.7 %select_maximum_fusion.2 = bf16[96,6,10,130]{3,2,1,0:T(8,128)(2,1)S(1)} fusion(bf16[97,1,8,128]{3,2,1,0:T(8,128)(2,1)} %collective-permute-done.1, bf16[97,1,8,128]{3,2,1,0:T(8,128)(2,1)} %collective-permute-done, bf16[1,4,8,128]{3,2,1,0:T(8,128)(2,1)S(1)} %bitcast.263, bf16[96,4,8,128]{3,2,1,0:T(8,128)(2,1)S(1)} %bitcast.241), kind=kLoop, calls=%fused_computation.29 | loop fusion | flops 17222400 | bytes 2689536 | tf_op jit(solution)/shard_map/concatenate | solution.py:26
  53.6 11.2 %fusion.22 = f32[96,4,8,128]{3,2,1,0:T(8,128)} fusion(bf16[96,4,8,128]{3,2,1,0:T(8,128)(2,1)S(1)} %bitcast.242, bf16[96,6,10,130]{3,2,1,0:T(8,128)(2,1)S(1)} %select_maximum_fusion.2, bf16[97,1,8,128]{3,2,1,0:T(8,128)(2,1)} %collective-permute-done.1, bf16[1,4,8,128]{3,2,1,0:T(8,128)(2,1)S(1)} %bitcast.264, bf16[97,1,8,128]{3,2,1,0:T(8,128)(2,1)} %collective-permute-done, ...), kind=kLoop, calls=%fused_computation.52 | loop fusion | flops 33030144 | bytes 22081536 | tf_op jit(solution)/shard_map/sub | solution.py:72
  72.8 2.4 copy.165
  75.4 12.8 %scatter_fusion = f32[96,4096]{0,1:T(8,128)S(1)} fusion(f32[96,4096]{0,1:T(8,128)S(1)} %bitcast.236, s32[2048]{0:T(1024)S(1)} %bitcast.267, f32[2048,96]{1,0:T(8,128)} %copy.165), kind=kCustom, calls=%fused_computation.2 | custom fusion | flops 196608 | bytes 2367488 | tf_op jit(solution)/shard_map/scatter-add | solution.py:80
  88.2 11.5 %scatter_fusion.1 = f32[4096]{0:T(1024)S(1)} fusion(f32[4096]{0:T(1024)S(1)} %copy.227, s32[2048]{0:T(1024)S(1)} %bitcast.268, f32[2048]{0:T(1024)S(1)} %fusion.69), kind=kCustom, calls=%fused_computation.3 | custom fusion | flops 2048 | bytes 32768 | tf_op jit(solution)/shard_map/scatter-add | solution.py:149
  99.7 4.6 fusion.78
  104.3 2.6 multiply_convert_fusion
  115.9 2.8 divide_convert_fusion.1
  120.9 2.9 collective-permute-start.3
  129.2 9.8 %gather_fusion.1 = bf16[2048,192]{1,0:T(8,128)(2,1)} fusion(bf16[192,4096]{0,1:T(8,128)(2,1)S(1)} %copy-done.1, s32[2048]{0:T(1024)} %copy-done.80), kind=kCustom, calls=%fused_computation.1 | custom fusion | bytes 1581056 | tf_op jit(solution)/shard_map/jit(_take)/gather | solution.py:118
  143.6 6.9 %all-to-all-start.1 = ((bf16[192,16,128]{2,0,1:T(8,128)(2,1)}), bf16[192,16,128]{2,0,1:T(8,128)(2,1)}, u32[]{:S(2)}, u32[]{:S(2)}) async-start(bf16[192,16,128]{2,0,1:T(8,128)(2,1)} %broadcast_select_fusion), calls=%async_computation.1 | async-start | bytes 1572864 | tf_op jit(solution)/shard_map/all_to_all | solution.py:119
  150.5 90.4 %all-reduce.15.cloned.1.call-done = f32[96,576]{1,0:T(8,128)} async-done(((f32[96,576]{1,0:T(8,128)}), f32[96,576]{1,0:T(8,128)}) %all-reduce.15.cloned.1.call-update) | async-done | bytes 221200 | tf_op jit(solution)/shard_map/psum | solution.py:171
  241.5 16.5 %select_maximum_fusion = bf16[192,6,10,130]{3,2,1,0:T(8,128)(2,1)S(1)} fusion(bf16[192,1,8,128]{3,2,1,0:T(8,128)(2,1)S(1)} %collective-permute-done.3, bf16[192,1,8,128]{3,2,1,0:T(8,128)(2,1)} %collective-permute-done.2, bf16[96,4,8,128]{3,2,1,0:T(8,128)(2,1)S(1)} %bitcast.253, bf16[96,4,8,128]{3,2,1,0:T(8,128)(2,1)S(1)} %copy-done.3), kind=kLoop, calls=%fused_computation.18 | loop fusion | flops 34444800 | bytes 5354496 | tf_op jit(solution)/shard_map/concatenate | solution.py:26
  258.3 27.3 %add_subtract_fusion = f32[192,4,8,128]{3,2,1,0:T(8,128)} fusion(bf16[96,4,8,128]{3,2,1,0:T(8,128)(2,1)S(1)} %bitcast.254, bf16[96,4,8,128]{3,2,1,0:T(8,128)(2,1)S(1)} %copy-done.3, bf16[192,6,10,130]{3,2,1,0:T(8,128)(2,1)S(1)} %select_maximum_fusion, bf16[192,1,8,128]{3,2,1,0:T(8,128)(2,1)S(1)} %collective-permute-done.3, ...), kind=kLoop, calls=%fused_computation.40 | loop fusion | flops 66846720 | bytes 43696128 | tf_op jit(solution)/shard_map/sub | solution.py:72
  285.5 5.1 copy.169
  290.6 2.6 fusion.26
  293.3 2.8 copy.172
  296.1 16.1 %scatter_fusion.2 = f32[192,4096]{0,1:T(8,128)} fusion(f32[192,4096]{0,1:T(8,128)} %bitcast.235, s32[2048]{0:T(1024)S(1)} %bitcast.269, f32[2048,192]{1,0:T(8,128)} %copy.172), kind=kCustom, calls=%fused_computation.4 | custom fusion | flops 393216 | bytes 4726784 | tf_op jit(solution)/shard_map/scatter-add | solution.py:80
  312.2 2.5 convert.18
  319.1 21.5 %all-reduce.17.cloned.1.call-done = f32[96,576]{1,0:T(8,128)} async-done(((f32[96,576]{1,0:T(8,128)}), f32[96,576]{1,0:T(8,128)}) %all-reduce.17.cloned.1.call-update) | async-done | bytes 221200 | tf_op jit(solution)/shard_map/psum | solution.py:171
  344.9 11.7 %cholesky.77 = f32[128,128]{1,0:T(8,128)S(1)} custom-call(f32[128,128]{1,0:T(8,128)S(1)} %copy.181), custom_call_target="Cholesky" | custom-call | tf_op jit(solution)/shard_map/jit(cholesky)/cholesky | solution.py:177
  356.7 9.8 %custom-call.22 = f32[1,128,128]{1,2,0:T(8,128)S(1)} custom-call(f32[1,128,128]{2,1,0:T(8,128)S(1)} %get-tuple-element.65), custom_call_target="InvertDiagBlocksLowerTriangular" | custom-call | tf_op jit(solution)/shard_map/jit(cholesky)/cholesky | solution.py:177
  367.3 11.7 %cholesky.162 = f32[128,128]{1,0:T(8,128)S(1)} custom-call(f32[128,128]{1,0:T(8,128)S(1)} %copy.183), custom_call_target="Cholesky" | custom-call | tf_op jit(solution)/shard_map/jit(cholesky)/cholesky | solution.py:177
  379.0 10.0 %custom-call.23 = f32[1,128,128]{1,2,0:T(8,128)S(1)} custom-call(f32[1,128,128]{2,1,0:T(8,128)S(1)} %get-tuple-element.62), custom_call_target="InvertDiagBlocksLowerTriangular" | custom-call | tf_op jit(solution)/shard_map/jit(cholesky)/cholesky | solution.py:177
  389.5 2.9 cholesky.184
  395.8 3.9 while.1
  399.8 29.5 %custom-call.24 = f32[3,128,128]{1,2,0:T(8,128)S(1)} custom-call(f32[3,128,128]{2,1,0:T(8,128)S(1)} %pad_maximum_fusion.18), custom_call_target="InvertDiagBlocksLowerTriangular" | custom-call | tf_op jit(solution)/shard_map/triangular_solve | solution.py:31
  431.3 17.1 %all-reduce.19.cloned.1.call-done = f32[96,576]{0,1:T(8,128)} async-done(((f32[96,576]{0,1:T(8,128)}), f32[96,576]{0,1:T(8,128)}) %all-reduce.19.cloned.1.call-update) | async-done | bytes 221200 | tf_op jit(solution)/shard_map/psum | solution.py:174
  448.6 98.1 %all-reduce.21.cloned.1.call-done = f32[96,576]{0,1:T(8,128)} async-done(((f32[96,576]{0,1:T(8,128)}), f32[96,576]{0,1:T(8,128)}) %all-reduce.21.cloned.1.call-update) | async-done | bytes 221200 | tf_op jit(solution)/shard_map/psum | solution.py:174
  (287 shorter events, 74.6 us)
Async XLA Ops:
  9.9 33.6 %collective-permute-start.1 = (bf16[97,1,8,128]{3,2,1,0:T(8,128)(2,1)}, bf16[97,1,8,128]{3,2,1,0:T(8,128)(2,1)}, u32[]{:S(2)}, u32[]{:S(2)}) collective-permute-start(bf16[97,1,8,128]{3,2,1,0:T(8,128)(2,1)} %get-tuple-element.60), channel_id=1, source_target_pairs={{1,0},{2,1},{3,2},{4,3},{5,4},{6,5},{7,6},{8,7},{9,8},{10,9},{11,1... | collective-permute-start | bytes 595976 | tf_op jit(solution)/shard_map/ppermute | solution.py:25
  11.8 31.7 %collective-permute-start = (bf16[97,1,8,128]{3,2,1,0:T(8,128)(2,1)}, bf16[97,1,8,128]{3,2,1,0:T(8,128)(2,1)}, u32[]{:S(2)}, u32[]{:S(2)}) collective-permute-start(bf16[97,1,8,128]{3,2,1,0:T(8,128)(2,1)} %get-tuple-element.59), channel_id=1, source_target_pairs={{0,1},{1,2},{2,3},{3,4},{4,5},{5,6},{6,7},{7,8},{8,9},{9,10},{10,1... | collective-permute-start | bytes 595976 | tf_op jit(solution)/shard_map/ppermute | solution.py:24
  18.3 69.9 %copy-start.21 = (s32[2048,1]{0,1:T(1,128)}, s32[2048,1]{0,1:T(1,128)S(1)}, u32[]{:S(2)}) copy-start(s32[2048,1]{0,1:T(1,128)S(1)} %compare_select_fusion) | copy-start | bytes 24580
  27.8 38.8 %all-to-all-start = ((bf16[97,16,128]{2,0,1:T(8,128)(2,1)}), bf16[97,16,128]{2,0,1:T(8,128)(2,1)}, u32[]{:S(2)}, u32[]{:S(2)}) async-start(bf16[97,16,128]{2,0,1:T(8,128)(2,1)} %broadcast_select_fusion.1), calls=%async_computation | async-start | bytes 851968 | tf_op jit(solution)/shard_map/all_to_all | solution.py:119
  34.9 206.0 %all-reduce.15.cloned.1.call-start = ((), (), s32[]{:S(2)}) async-start(), calls=%async_computation.2 | async-start | bytes 491520 | tf_op jit(solution)/shard_map/psum | solution.py:171
  70.8 17.3 %copy-start.77 = (f32[2048]{0:T(1024)}, f32[2048]{0:T(1024)S(1)}, u32[]{:S(2)}) copy-start(f32[2048]{0:T(1024)S(1)} %get-tuple-element.15) | copy-start | bytes 24580
  120.9 120.5 %collective-permute-start.3 = (bf16[192,1,8,128]{3,2,1,0:T(8,128)(2,1)}, bf16[192,1,8,128]{3,2,1,0:T(8,128)(2,1)S(1)}, u32[]{:S(2)}, u32[]{:S(2)}) collective-permute-start(bf16[192,1,8,128]{3,2,1,0:T(8,128)(2,1)} %get-tuple-element.58), channel_id=1, source_target_pairs={{1,0},{2,1},{3,2},{4,3},{5,4},{6,5},{7,6},{8,7},{9,8},{10,9},{11,1... | collective-permute-start | bytes 1179656 | tf_op jit(solution)/shard_map/ppermute | solution.py:25
  123.8 117.7 %collective-permute-start.2 = (bf16[192,1,8,128]{3,2,1,0:T(8,128)(2,1)}, bf16[192,1,8,128]{3,2,1,0:T(8,128)(2,1)}, u32[]{:S(2)}, u32[]{:S(2)}) collective-permute-start(bf16[192,1,8,128]{3,2,1,0:T(8,128)(2,1)} %get-tuple-element.57), channel_id=1, source_target_pairs={{0,1},{1,2},{2,3},{3,4},{4,5},{5,6},{6,7},{7,8},{8,9},{9,10},{10,1... | collective-permute-start | bytes 1179656 | tf_op jit(solution)/shard_map/ppermute | solution.py:24
  139.0 102.4 %copy-start.3 = (bf16[96,4,8,128]{3,2,1,0:T(8,128)(2,1)S(1)}, bf16[96,4,8,128]{3,2,1,0:T(8,128)(2,1)}, u32[]{:S(2)}) copy-start(bf16[96,4,8,128]{3,2,1,0:T(8,128)(2,1)} %copy-done.2) | copy-start | bytes 2359300
  139.0 102.5 %copy-start.11 = (bf16[96,1,4,8,128]{4,3,2,1,0:T(8,128)(2,1)S(1)}, bf16[96,1,4,8,128]{4,3,2,1,0:T(8,128)(2,1)}, u32[]{:S(2)}) copy-start(bf16[96,1,4,8,128]{4,3,2,1,0:T(8,128)(2,1)} %param.9) | copy-start | bytes 2359300
  143.6 147.1 %all-to-all-start.1 = ((bf16[192,16,128]{2,0,1:T(8,128)(2,1)}), bf16[192,16,128]{2,0,1:T(8,128)(2,1)}, u32[]{:S(2)}, u32[]{:S(2)}) async-start(bf16[192,16,128]{2,0,1:T(8,128)(2,1)} %broadcast_select_fusion), calls=%async_computation.1 | async-start | bytes 1572864 | tf_op jit(solution)/shard_map/all_to_all | solution.py:119
  150.5 190.1 %all-reduce.17.cloned.1.call-start = ((), (), s32[]{:S(2)}) async-start(), calls=%async_computation.3 | async-start | bytes 491520 | tf_op jit(solution)/shard_map/psum | solution.py:171
  240.9 17.1 %copy-start.24 = (f32[4,8,128]{2,1,0:T(8,128)S(1)}, f32[4,8,128]{2,1,0:T(8,128)}, u32[]{:S(2)}) copy-start(f32[4,8,128]{2,1,0:T(8,128)} %copy-done.23) | copy-start | bytes 49156
  240.9 17.1 %copy-start.26 = (f32[4,8,128]{2,1,0:T(8,128)S(1)}, f32[4,8,128]{2,1,0:T(8,128)}, u32[]{:S(2)}) copy-start(f32[4,8,128]{2,1,0:T(8,128)} %copy-done.25) | copy-start | bytes 49156
  240.9 17.1 %copy-start.28 = (f32[4,8,128]{2,1,0:T(8,128)S(1)}, f32[4,8,128]{2,1,0:T(8,128)}, u32[]{:S(2)}) copy-start(f32[4,8,128]{2,1,0:T(8,128)} %copy-done.27) | copy-start | bytes 49156
  241.0 17.1 %copy-start.30 = (f32[4,8,128]{2,1,0:T(8,128)S(1)}, f32[4,8,128]{2,1,0:T(8,128)}, u32[]{:S(2)}) copy-start(f32[4,8,128]{2,1,0:T(8,128)} %copy-done.29) | copy-start | bytes 49156
  241.0 17.1 %copy-start.32 = (f32[4,8,128]{2,1,0:T(8,128)S(1)}, f32[4,8,128]{2,1,0:T(8,128)}, u32[]{:S(2)}) copy-start(f32[4,8,128]{2,1,0:T(8,128)} %copy-done.31) | copy-start | bytes 49156
  241.0 17.1 %copy-start.34 = (f32[4,8,128]{2,1,0:T(8,128)S(1)}, f32[4,8,128]{2,1,0:T(8,128)}, u32[]{:S(2)}) copy-start(f32[4,8,128]{2,1,0:T(8,128)} %copy-done.33) | copy-start | bytes 49156
  241.0 17.1 %copy-start.36 = (f32[4,8,128]{2,1,0:T(8,128)S(1)}, f32[4,8,128]{2,1,0:T(8,128)}, u32[]{:S(2)}) copy-start(f32[4,8,128]{2,1,0:T(8,128)} %copy-done.35) | copy-start | bytes 49156
  241.0 17.1 %copy-start.38 = (f32[4,8,128]{2,1,0:T(8,128)S(1)}, f32[4,8,128]{2,1,0:T(8,128)}, u32[]{:S(2)}) copy-start(f32[4,8,128]{2,1,0:T(8,128)} %copy-done.37) | copy-start | bytes 49156
  241.0 17.1 %copy-start.40 = (f32[4,8,128]{2,1,0:T(8,128)S(1)}, f32[4,8,128]{2,1,0:T(8,128)}, u32[]{:S(2)}) copy-start(f32[4,8,128]{2,1,0:T(8,128)} %copy-done.39) | copy-start | bytes 49156
  241.0 17.1 %copy-start.42 = (f32[4,8,128]{2,1,0:T(8,128)S(1)}, f32[4,8,128]{2,1,0:T(8,128)}, u32[]{:S(2)}) copy-start(f32[4,8,128]{2,1,0:T(8,128)} %copy-done.41) | copy-start | bytes 49156
  241.0 17.1 %copy-start.44 = (f32[4,8,128]{2,1,0:T(8,128)S(1)}, f32[4,8,128]{2,1,0:T(8,128)}, u32[]{:S(2)}) copy-start(f32[4,8,128]{2,1,0:T(8,128)} %copy-done.43) | copy-start | bytes 49156
  241.0 17.1 %copy-start.46 = (f32[4,8,128]{2,1,0:T(8,128)S(1)}, f32[4,8,128]{2,1,0:T(8,128)}, u32[]{:S(2)}) copy-start(f32[4,8,128]{2,1,0:T(8,128)} %copy-done.45) | copy-start | bytes 49156
  241.0 17.1 %copy-start.48 = (f32[4,8,128]{2,1,0:T(8,128)S(1)}, f32[4,8,128]{2,1,0:T(8,128)}, u32[]{:S(2)}) copy-start(f32[4,8,128]{2,1,0:T(8,128)} %copy-done.47) | copy-start | bytes 49156
  241.2 207.1 %all-reduce.19.cloned.1.call-start = ((), (), s32[]{:S(2)}) async-start(), calls=%async_computation.4 | async-start | bytes 589824 | tf_op jit(solution)/shard_map/psum | solution.py:174
  317.5 26.8 %copy-start.83 = (s32[288]{0:T(512)S(1)}, s32[288]{0:T(512)}, u32[]{:S(2)}) copy-start(s32[288]{0:T(512)} %iota_add_fusion) | copy-start | bytes 3460
  343.6 203.2 %all-reduce.21.cloned.1.call-start = ((), (), s32[]{:S(2)}) async-start(), calls=%async_computation.5 | async-start | bytes 589824 | tf_op jit(solution)/shard_map/psum | solution.py:174
  344.7 51.0 %copy-start.87 = (s32[2]{0:T(128)S(1)}, s32[2]{0:T(128)}, u32[]{:S(2)}) copy-start(s32[2]{0:T(128)} %iota_multiply_fusion) | copy-start | bytes 28
  344.7 51.1 %copy-start.76 = (f32[2,128,128]{2,1,0:T(8,128)S(1)}, f32[2,128,128]{2,1,0:T(8,128)}, u32[]{:S(2)}) copy-start(f32[2,128,128]{2,1,0:T(8,128)} %custom-call.29) | copy-start | bytes 393220
  344.8 54.9 %copy-start.20 = (f32[128,96]{1,0:T(8,128)S(1)}, f32[128,96]{1,0:T(8,128)}, u32[]{:S(2)}) copy-start(f32[128,96]{1,0:T(8,128)} %pad_convert_fusion) | copy-start | bytes 147460
  356.6 73.7 %copy-start.17 = (f32[288,288]{0,1:T(8,128)S(1)}, f32[288,288]{0,1:T(8,128)}, u32[]{:S(2)}) copy-start(f32[288,288]{0,1:T(8,128)} %fusion.57) | copy-start | bytes 995332
  (66 other events, 630.2 us)
Sparse Core Ops, SparseCore 0:
  129.4 111.4 all-reduce.14
  244.1 96.5 all-reduce.16
  343.7 104.5 all-reduce.18
  451.4 95.2 all-reduce.20
where the time goes:
time: 569 us; the launch traced here: 560 us
  waiting for transfers between devices  227 us (40%)
  other arithmetic  219 us (38%)
  local copies, waits for them, and re-layouts  56 us (10%)
  starting transfers between devices  24.2 us (4%)
  between operations  17.4 us (3%)
  matrix products  16 us (3%)
    psum x2, waiting for transfers between devices, on_device(): gram_k = lax.psum(lax.psum(stiff_part, 'bulk'), 'sec')  115 us
    psum x1, waiting for transfers between devices, on_device(): lax.psum(upper_blocks(span, mass_span, modes), 'bulk')  90.4 us
    another operation x10, other arithmetic, on_device(): lower = jnp.linalg.cholesky(mass_gram)  47.6 us
    sub x2, other arithmetic, apply_stencil(): return summed[None] * centre - accum  38.4 us
    another operation x7, other arithmetic, lower_solve(): lax.linalg.triangular_solve(lower, matrix, left_side=True, lower=True)  30.8 us
    scatter-add x2, other arithmetic, joint_apply(): result.reshape(width, -1).at[:, node_ids].add(delta).reshape(result.shape)  28.9 us
    concatenate x2, other arithmetic, extended(): shard = jnp.concatenate([before, shard, after], axis=dim)  25.2 us
    psum x1, waiting for transfers between devices, on_device(): lax.psum(lax.psum(upper_blocks(span, mass_span, modes), 'bulk'), 'sec')  21.5 us
  transfers between devices with their start and end apart: 10, of which 4 were waited for; matrix products, arithmetic and copies ran while one was open for 40% of the time, Pallas kernels for 0%

commit v1 on v0

--- a/solution.py
+++ b/solution.py
@@ -168,7 +168,9 @@
         jnp.concatenate([stiff_first, stiff_wp], axis=0).astype(jnp.bfloat16).reshape(columns, -1)
     )
     mass_span = (mass.reshape(1, -1) * span.astype(jnp.float32)).astype(jnp.bfloat16)
-    gram_m = lax.psum(lax.psum(upper_blocks(span, mass_span, modes), "bulk"), "sec")
+    gram_m = jnp.sum(
+        lax.all_gather(lax.psum(upper_blocks(span, mass_span, modes), "bulk"), "sec"), axis=0
+    )
     stiff_part = upper_blocks(span, stiff_span, modes)
     gram_m, stiff_part = lax.optimization_barrier((gram_m, stiff_part))
     gram_k = lax.psum(lax.psum(stiff_part, "bulk"), "sec")

time: 569 us -> 559 us (0.982)
    psum x1 -> x0, waiting for transfers between devices: 21.5 us -> none  [on_device(): lax.psum(lax.psum(upper_blocks(span, mass_span, modes), 'bulk'), 'sec')]
    psum x2, waiting for transfers between devices: 115 us -> 130 us  [on_device(): gram_k = lax.psum(lax.psum(stiff_part, 'bulk'), 'sec')]
  transfers between devices with their start and end apart: 10 -> 10, of which waited for: 4 -> 3; matrix products, arithmetic and copies ran while one was open for 40% -> 38% of each run, Pallas kernels for 0% -> 0%
where the time goes in v1:
time: 559 us; the launch traced here: 550 us
  waiting for transfers between devices  223 us (40%)
  other arithmetic  219 us (39%)
  local copies, waits for them, and re-layouts  51.7 us (9%)
  starting transfers between devices  23.9 us (4%)
  between operations  17.7 us (3%)
  matrix products  14.7 us (3%)
    psum x2, waiting for transfers between devices, on_device(): gram_k = lax.psum(lax.psum(stiff_part, 'bulk'), 'sec')  130 us
    psum x1, waiting for transfers between devices, on_device(): lax.psum(upper_blocks(span, mass_span, modes), 'bulk')  92.7 us
    another operation x10, other arithmetic, on_device(): lower = jnp.linalg.cholesky(mass_gram)  47.5 us
    sub x2, other arithmetic, apply_stencil(): return summed[None] * centre - accum  38.4 us
    another operation x7, other arithmetic, lower_solve(): lax.linalg.triangular_solve(lower, matrix, left_side=True, lower=True)  30.8 us
    scatter-add x2, other arithmetic, joint_apply(): result.reshape(width, -1).at[:, node_ids].add(delta).reshape(result.shape)  28.9 us
    concatenate x2, other arithmetic, extended(): shard = jnp.concatenate([before, shard, after], axis=dim)  25.2 us
    gather x4, local copies, waits for them, and re-layouts, fetch(): jnp.take(block.reshape(width, -1), node_ids, axis=1)  17.2 us
  transfers between devices with their start and end apart: 10, of which 3 were waited for; matrix products, arithmetic and copies ran while one was open for 38% of the time, Pallas kernels for 0%

profile of v1, /device:TPU:32, one launch (start us, length us, event | category | flops | bytes accessed | tf_op | source)
XLA Modules:
  0.0 550.3 jit_solution(3170817346446067639)
XLA Ops:
  11.8 2.4 collective-permute-start
  14.2 3.2 convert_element_type.358
  20.4 6.2 %gather_fusion = bf16[2048,97]{1,0:T(8,128)(2,1)S(1)} fusion(bf16[97,4096]{0,1:T(8,128)(2,1)S(1)} %pad_maximum_fusion.6, s32[2048]{0:T(1024)S(1)} %broadcast_clamp_fusion), kind=kCustom, calls=%fused_computation | custom fusion | bytes 802816 | tf_op jit(solution)/shard_map/jit(_take)/gather | solution.py:118
  27.8 7.1 %all-to-all-start = ((bf16[97,16,128]{2,0,1:T(8,128)(2,1)}), bf16[97,16,128]{2,0,1:T(8,128)(2,1)}, u32[]{:S(2)}, u32[]{:S(2)}) async-start(bf16[97,16,128]{2,0,1:T(8,128)(2,1)} %broadcast_select_fusion.1), calls=%async_computation | async-start | bytes 851968 | tf_op jit(solution)/shard_map/all_to_all | solution.py:119
  44.5 8.7 %select_maximum_fusion.2 = bf16[96,6,10,130]{3,2,1,0:T(8,128)(2,1)S(1)} fusion(bf16[97,1,8,128]{3,2,1,0:T(8,128)(2,1)} %collective-permute-done.1, bf16[97,1,8,128]{3,2,1,0:T(8,128)(2,1)} %collective-permute-done, bf16[1,4,8,128]{3,2,1,0:T(8,128)(2,1)S(1)} %bitcast.265, bf16[96,4,8,128]{3,2,1,0:T(8,128)(2,1)S(1)} %bitcast.243), kind=kLoop, calls=%fused_computation.29 | loop fusion | flops 17222400 | bytes 2689536 | tf_op jit(solution)/shard_map/concatenate | solution.py:26
  53.4 11.2 %fusion.22 = f32[96,4,8,128]{3,2,1,0:T(8,128)} fusion(bf16[96,4,8,128]{3,2,1,0:T(8,128)(2,1)S(1)} %bitcast.244, bf16[96,6,10,130]{3,2,1,0:T(8,128)(2,1)S(1)} %select_maximum_fusion.2, bf16[97,1,8,128]{3,2,1,0:T(8,128)(2,1)} %collective-permute-done.1, bf16[1,4,8,128]{3,2,1,0:T(8,128)(2,1)S(1)} %bitcast.266, bf16[97,1,8,128]{3,2,1,0:T(8,128)(2,1)} %collective-permute-done, ...), kind=kLoop, calls=%fused_computation.52 | loop fusion | flops 33030144 | bytes 22081536 | tf_op jit(solution)/shard_map/sub | solution.py:72
  72.7 2.5 copy.165
  75.3 12.8 %scatter_fusion = f32[96,4096]{0,1:T(8,128)S(1)} fusion(f32[96,4096]{0,1:T(8,128)S(1)} %bitcast.238, s32[2048]{0:T(1024)S(1)} %bitcast.269, f32[2048,96]{1,0:T(8,128)} %copy.165), kind=kCustom, calls=%fused_computation.2 | custom fusion | flops 196608 | bytes 2367488 | tf_op jit(solution)/shard_map/scatter-add | solution.py:80
  88.1 11.5 %scatter_fusion.1 = f32[4096]{0:T(1024)S(1)} fusion(f32[4096]{0:T(1024)S(1)} %copy.228, s32[2048]{0:T(1024)S(1)} %bitcast.270, f32[2048]{0:T(1024)S(1)} %fusion.69), kind=kCustom, calls=%fused_computation.3 | custom fusion | flops 2048 | bytes 32768 | tf_op jit(solution)/shard_map/scatter-add | solution.py:149
  99.7 4.6 fusion.78
  104.3 2.6 multiply_convert_fusion
  114.6 2.8 divide_convert_fusion.1
  119.6 2.9 collective-permute-start.3
  124.7 2.4 convolution_bitcast_fusion.3
  128.0 9.0 %gather_fusion.1 = bf16[2048,192]{1,0:T(8,128)(2,1)} fusion(bf16[192,4096]{0,1:T(8,128)(2,1)S(1)} %copy-done.1, s32[2048]{0:T(1024)S(1)} %copy-done.79), kind=kCustom, calls=%fused_computation.1 | custom fusion | bytes 1581056 | tf_op jit(solution)/shard_map/jit(_take)/gather | solution.py:118
  139.7 6.9 %all-to-all-start.1 = ((bf16[192,16,128]{2,0,1:T(8,128)(2,1)}), bf16[192,16,128]{2,0,1:T(8,128)(2,1)S(1)}, u32[]{:S(2)}, u32[]{:S(2)}) async-start(bf16[192,16,128]{2,0,1:T(8,128)(2,1)} %broadcast_select_fusion), calls=%async_computation.1 | async-start | bytes 1572864 | tf_op jit(solution)/shard_map/all_to_all | solution.py:119
  146.7 92.7 %all-reduce.14.cloned.1.call-done = f32[1,96,576]{2,1,0:T(8,128)} async-done(((f32[1,96,576]{2,1,0:T(8,128)}), f32[1,96,576]{2,1,0:T(8,128)}) %all-reduce.14.cloned.1.call-update) | async-done | bytes 221200 | tf_op jit(solution)/shard_map/psum | solution.py:172
  240.0 16.5 %select_maximum_fusion = bf16[192,6,10,130]{3,2,1,0:T(8,128)(2,1)S(1)} fusion(bf16[192,1,8,128]{3,2,1,0:T(8,128)(2,1)S(1)} %collective-permute-done.3, bf16[192,1,8,128]{3,2,1,0:T(8,128)(2,1)} %collective-permute-done.2, bf16[96,4,8,128]{3,2,1,0:T(8,128)(2,1)S(1)} %bitcast.255, bf16[96,4,8,128]{3,2,1,0:T(8,128)(2,1)S(1)} %copy-done.3), kind=kLoop, calls=%fused_computation.18 | loop fusion | flops 34444800 | bytes 5354496 | tf_op jit(solution)/shard_map/concatenate | solution.py:26
  256.8 27.2 %add_subtract_fusion = f32[192,4,8,128]{3,2,1,0:T(8,128)} fusion(bf16[96,4,8,128]{3,2,1,0:T(8,128)(2,1)S(1)} %bitcast.256, bf16[96,4,8,128]{3,2,1,0:T(8,128)(2,1)S(1)} %copy-done.3, bf16[192,6,10,130]{3,2,1,0:T(8,128)(2,1)S(1)} %select_maximum_fusion, bf16[192,1,8,128]{3,2,1,0:T(8,128)(2,1)S(1)} %collective-permute-done.3, ...), kind=kLoop, calls=%fused_computation.40 | loop fusion | flops 66846720 | bytes 43696128 | tf_op jit(solution)/shard_map/sub | solution.py:72
  284.0 5.0 copy.169
  292.3 16.1 %scatter_fusion.2 = f32[192,4096]{0,1:T(8,128)} fusion(f32[192,4096]{0,1:T(8,128)} %bitcast.237, s32[2048]{0:T(1024)S(1)} %bitcast.271, f32[2048,192]{1,0:T(8,128)S(1)} %copy.172), kind=kCustom, calls=%fused_computation.4 | custom fusion | flops 393216 | bytes 4726784 | tf_op jit(solution)/shard_map/scatter-add | solution.py:80
  308.4 2.4 convert.18
  315.6 2.3 reduce_sum.29
  319.0 11.7 %cholesky.77 = f32[128,128]{1,0:T(8,128)S(1)} custom-call(f32[128,128]{1,0:T(8,128)S(1)} %copy.181), custom_call_target="Cholesky" | custom-call | tf_op jit(solution)/shard_map/jit(cholesky)/cholesky | solution.py:179
  331.0 9.8 %custom-call.22 = f32[1,128,128]{1,2,0:T(8,128)S(1)} custom-call(f32[1,128,128]{2,1,0:T(8,128)S(1)} %get-tuple-element.65), custom_call_target="InvertDiagBlocksLowerTriangular" | custom-call | tf_op jit(solution)/shard_map/jit(cholesky)/cholesky | solution.py:179
  341.6 11.7 %cholesky.162 = f32[128,128]{1,0:T(8,128)S(1)} custom-call(f32[128,128]{1,0:T(8,128)S(1)} %copy.183), custom_call_target="Cholesky" | custom-call | tf_op jit(solution)/shard_map/jit(cholesky)/cholesky | solution.py:179
  353.4 9.8 %custom-call.23 = f32[1,128,128]{1,2,0:T(8,128)S(1)} custom-call(f32[1,128,128]{2,1,0:T(8,128)S(1)} %get-tuple-element.62), custom_call_target="InvertDiagBlocksLowerTriangular" | custom-call | tf_op jit(solution)/shard_map/jit(cholesky)/cholesky | solution.py:179
  363.7 2.9 cholesky.184
  370.3 4.5 while.1
  374.9 29.5 %custom-call.24 = f32[3,128,128]{1,2,0:T(8,128)S(1)} custom-call(f32[3,128,128]{2,1,0:T(8,128)S(1)} %pad_maximum_fusion.17), custom_call_target="InvertDiagBlocksLowerTriangular" | custom-call | tf_op jit(solution)/shard_map/triangular_solve | solution.py:31
  406.4 31.7 %all-reduce.16.cloned.1.call-done = f32[96,576]{0,1:T(8,128)} async-done(((f32[96,576]{0,1:T(8,128)}), f32[96,576]{0,1:T(8,128)}) %all-reduce.16.cloned.1.call-update) | async-done | bytes 221200 | tf_op jit(solution)/shard_map/psum | solution.py:176
  438.4 98.4 %all-reduce.18.cloned.1.call-done = f32[96,576]{0,1:T(8,128)} async-done(((f32[96,576]{0,1:T(8,128)}), f32[96,576]{0,1:T(8,128)}) %all-reduce.18.cloned.1.call-update) | async-done | bytes 221200 | tf_op jit(solution)/shard_map/psum | solution.py:176
  (288 shorter events, 67.8 us)
Async XLA Ops:
  9.9 33.5 %collective-permute-start.1 = (bf16[97,1,8,128]{3,2,1,0:T(8,128)(2,1)}, bf16[97,1,8,128]{3,2,1,0:T(8,128)(2,1)}, u32[]{:S(2)}, u32[]{:S(2)}) collective-permute-start(bf16[97,1,8,128]{3,2,1,0:T(8,128)(2,1)} %get-tuple-element.60), channel_id=1, source_target_pairs={{1,0},{2,1},{3,2},{4,3},{5,4},{6,5},{7,6},{8,7},{9,8},{10,9},{11,1... | collective-permute-start | bytes 595976 | tf_op jit(solution)/shard_map/ppermute | solution.py:25
  11.8 31.5 %collective-permute-start = (bf16[97,1,8,128]{3,2,1,0:T(8,128)(2,1)}, bf16[97,1,8,128]{3,2,1,0:T(8,128)(2,1)}, u32[]{:S(2)}, u32[]{:S(2)}) collective-permute-start(bf16[97,1,8,128]{3,2,1,0:T(8,128)(2,1)} %get-tuple-element.59), channel_id=1, source_target_pairs={{0,1},{1,2},{2,3},{3,4},{4,5},{5,6},{6,7},{7,8},{8,9},{9,10},{10,1... | collective-permute-start | bytes 595976 | tf_op jit(solution)/shard_map/ppermute | solution.py:24
  18.3 69.8 %copy-start.20 = (s32[2048,1]{0,1:T(1,128)}, s32[2048,1]{0,1:T(1,128)S(1)}, u32[]{:S(2)}) copy-start(s32[2048,1]{0,1:T(1,128)S(1)} %compare_select_fusion) | copy-start | bytes 24580
  27.8 38.7 %all-to-all-start = ((bf16[97,16,128]{2,0,1:T(8,128)(2,1)}), bf16[97,16,128]{2,0,1:T(8,128)(2,1)}, u32[]{:S(2)}, u32[]{:S(2)}) async-start(bf16[97,16,128]{2,0,1:T(8,128)(2,1)} %broadcast_select_fusion.1), calls=%async_computation | async-start | bytes 851968 | tf_op jit(solution)/shard_map/all_to_all | solution.py:119
  34.9 204.5 %all-reduce.14.cloned.1.call-start = ((), (), s32[]{:S(2)}) async-start(), calls=%async_computation.2 | async-start | bytes 491520 | tf_op jit(solution)/shard_map/psum | solution.py:172
  70.7 17.4 %copy-start.75 = (f32[2048]{0:T(1024)}, f32[2048]{0:T(1024)S(1)}, u32[]{:S(2)}) copy-start(f32[2048]{0:T(1024)S(1)} %get-tuple-element.15) | copy-start | bytes 24580
  119.6 120.3 %collective-permute-start.3 = (bf16[192,1,8,128]{3,2,1,0:T(8,128)(2,1)}, bf16[192,1,8,128]{3,2,1,0:T(8,128)(2,1)S(1)}, u32[]{:S(2)}, u32[]{:S(2)}) collective-permute-start(bf16[192,1,8,128]{3,2,1,0:T(8,128)(2,1)} %get-tuple-element.58), channel_id=1, source_target_pairs={{1,0},{2,1},{3,2},{4,3},{5,4},{6,5},{7,6},{8,7},{9,8},{10,9},{11,1... | collective-permute-start | bytes 1179656 | tf_op jit(solution)/shard_map/ppermute | solution.py:25
  122.5 117.4 %collective-permute-start.2 = (bf16[192,1,8,128]{3,2,1,0:T(8,128)(2,1)}, bf16[192,1,8,128]{3,2,1,0:T(8,128)(2,1)}, u32[]{:S(2)}, u32[]{:S(2)}) collective-permute-start(bf16[192,1,8,128]{3,2,1,0:T(8,128)(2,1)} %get-tuple-element.57), channel_id=1, source_target_pairs={{0,1},{1,2},{2,3},{3,4},{4,5},{5,6},{6,7},{7,8},{8,9},{9,10},{10,1... | collective-permute-start | bytes 1179656 | tf_op jit(solution)/shard_map/ppermute | solution.py:24
  137.0 102.9 %copy-start.3 = (bf16[96,4,8,128]{3,2,1,0:T(8,128)(2,1)S(1)}, bf16[96,4,8,128]{3,2,1,0:T(8,128)(2,1)}, u32[]{:S(2)}) copy-start(bf16[96,4,8,128]{3,2,1,0:T(8,128)(2,1)} %copy-done.2) | copy-start | bytes 2359300
  137.0 102.9 %copy-start.12 = (bf16[96,1,4,8,128]{4,3,2,1,0:T(8,128)(2,1)S(1)}, bf16[96,1,4,8,128]{4,3,2,1,0:T(8,128)(2,1)}, u32[]{:S(2)}) copy-start(bf16[96,1,4,8,128]{4,3,2,1,0:T(8,128)(2,1)} %param.9) | copy-start | bytes 2359300
  139.7 149.3 %all-to-all-start.1 = ((bf16[192,16,128]{2,0,1:T(8,128)(2,1)}), bf16[192,16,128]{2,0,1:T(8,128)(2,1)S(1)}, u32[]{:S(2)}, u32[]{:S(2)}) async-start(bf16[192,16,128]{2,0,1:T(8,128)(2,1)} %broadcast_select_fusion), calls=%async_computation.1 | async-start | bytes 1572864 | tf_op jit(solution)/shard_map/all_to_all | solution.py:119
  146.6 168.9 %all-gather.2.cloned.1.call-start = ((), (), s32[]{:S(2)}) async-start(), calls=%async_computation.3 | async-start | bytes 4177920 | tf_op jit(solution)/shard_map/all_gather | solution.py:172
  239.4 198.7 %all-reduce.16.cloned.1.call-start = ((), (), s32[]{:S(2)}) async-start(), calls=%async_computation.4 | async-start | bytes 589824 | tf_op jit(solution)/shard_map/psum | solution.py:176
  239.7 16.8 %copy-start.23 = (f32[4,8,128]{2,1,0:T(8,128)S(1)}, f32[4,8,128]{2,1,0:T(8,128)}, u32[]{:S(2)}) copy-start(f32[4,8,128]{2,1,0:T(8,128)} %copy-done.22) | copy-start | bytes 49156
  239.7 16.8 %copy-start.25 = (f32[4,8,128]{2,1,0:T(8,128)S(1)}, f32[4,8,128]{2,1,0:T(8,128)}, u32[]{:S(2)}) copy-start(f32[4,8,128]{2,1,0:T(8,128)} %copy-done.24) | copy-start | bytes 49156
  239.7 16.8 %copy-start.27 = (f32[4,8,128]{2,1,0:T(8,128)S(1)}, f32[4,8,128]{2,1,0:T(8,128)}, u32[]{:S(2)}) copy-start(f32[4,8,128]{2,1,0:T(8,128)} %copy-done.26) | copy-start | bytes 49156
  239.7 16.8 %copy-start.29 = (f32[4,8,128]{2,1,0:T(8,128)S(1)}, f32[4,8,128]{2,1,0:T(8,128)}, u32[]{:S(2)}) copy-start(f32[4,8,128]{2,1,0:T(8,128)} %copy-done.28) | copy-start | bytes 49156
  239.7 16.8 %copy-start.31 = (f32[4,8,128]{2,1,0:T(8,128)S(1)}, f32[4,8,128]{2,1,0:T(8,128)}, u32[]{:S(2)}) copy-start(f32[4,8,128]{2,1,0:T(8,128)} %copy-done.30) | copy-start | bytes 49156
  239.7 16.8 %copy-start.33 = (f32[4,8,128]{2,1,0:T(8,128)S(1)}, f32[4,8,128]{2,1,0:T(8,128)}, u32[]{:S(2)}) copy-start(f32[4,8,128]{2,1,0:T(8,128)} %copy-done.32) | copy-start | bytes 49156
  239.7 16.8 %copy-start.35 = (f32[4,8,128]{2,1,0:T(8,128)S(1)}, f32[4,8,128]{2,1,0:T(8,128)}, u32[]{:S(2)}) copy-start(f32[4,8,128]{2,1,0:T(8,128)} %copy-done.34) | copy-start | bytes 49156
  239.7 16.8 %copy-start.37 = (f32[4,8,128]{2,1,0:T(8,128)S(1)}, f32[4,8,128]{2,1,0:T(8,128)}, u32[]{:S(2)}) copy-start(f32[4,8,128]{2,1,0:T(8,128)} %copy-done.36) | copy-start | bytes 49156
  239.8 16.8 %copy-start.39 = (f32[4,8,128]{2,1,0:T(8,128)S(1)}, f32[4,8,128]{2,1,0:T(8,128)}, u32[]{:S(2)}) copy-start(f32[4,8,128]{2,1,0:T(8,128)} %copy-done.38) | copy-start | bytes 49156
  239.8 16.8 %copy-start.41 = (f32[4,8,128]{2,1,0:T(8,128)S(1)}, f32[4,8,128]{2,1,0:T(8,128)}, u32[]{:S(2)}) copy-start(f32[4,8,128]{2,1,0:T(8,128)} %copy-done.40) | copy-start | bytes 49156
  239.8 16.8 %copy-start.43 = (f32[4,8,128]{2,1,0:T(8,128)S(1)}, f32[4,8,128]{2,1,0:T(8,128)}, u32[]{:S(2)}) copy-start(f32[4,8,128]{2,1,0:T(8,128)} %copy-done.42) | copy-start | bytes 49156
  239.8 16.8 %copy-start.45 = (f32[4,8,128]{2,1,0:T(8,128)S(1)}, f32[4,8,128]{2,1,0:T(8,128)}, u32[]{:S(2)}) copy-start(f32[4,8,128]{2,1,0:T(8,128)} %copy-done.44) | copy-start | bytes 49156
  239.8 16.8 %copy-start.47 = (f32[4,8,128]{2,1,0:T(8,128)S(1)}, f32[4,8,128]{2,1,0:T(8,128)}, u32[]{:S(2)}) copy-start(f32[4,8,128]{2,1,0:T(8,128)} %copy-done.46) | copy-start | bytes 49156
  239.8 16.8 %copy-start.49 = (f32[4,8,128]{2,1,0:T(8,128)S(1)}, f32[4,8,128]{2,1,0:T(8,128)}, u32[]{:S(2)}) copy-start(f32[4,8,128]{2,1,0:T(8,128)} %copy-done.48) | copy-start | bytes 49156
  318.8 51.4 %copy-start.87 = (s32[2]{0:T(128)S(1)}, s32[2]{0:T(128)}, u32[]{:S(2)}) copy-start(s32[2]{0:T(128)} %iota_multiply_fusion) | copy-start | bytes 28
  318.8 51.5 %copy-start.74 = (f32[2,128,128]{2,1,0:T(8,128)S(1)}, f32[2,128,128]{2,1,0:T(8,128)}, u32[]{:S(2)}) copy-start(f32[2,128,128]{2,1,0:T(8,128)} %custom-call.29) | copy-start | bytes 393220
  318.9 56.0 %copy-start.19 = (f32[128,96]{1,0:T(8,128)S(1)}, f32[128,96]{1,0:T(8,128)}, u32[]{:S(2)}) copy-start(f32[128,96]{1,0:T(8,128)} %pad_convert_fusion) | copy-start | bytes 147460
  330.7 74.7 %copy-start.17 = (f32[288,288]{0,1:T(8,128)S(1)}, f32[288,288]{0,1:T(8,128)}, u32[]{:S(2)}) copy-start(f32[288,288]{0,1:T(8,128)} %fusion.57) | copy-start | bytes 995332
  330.8 206.0 %all-reduce.18.cloned.1.call-start = ((), (), s32[]{:S(2)}) async-start(), calls=%async_computation.5 | async-start | bytes 589824 | tf_op jit(solution)/shard_map/psum | solution.py:176
  (66 other events, 605.7 us)
Sparse Core Ops, SparseCore 0:
  128.1 111.2 all-reduce.13
  241.8 56.9 all-gather.1
  330.9 107.1 all-reduce.15
  441.2 95.5 all-reduce.17
